TPU v7x, 32 devices: a whole 2x2x4 slice. The times are simulated.
32 devices in a mesh: grp: 4 (over z), mem: 8 (over y, x, core).
Axes of the slice: x: 2, y: 2, z: 4, core: 2. Of those that a mesh axis runs over, the one named last changes fastest.
Arguments:
- design: bfloat16 [8192, 1024], P(('grp', 'mem'))
- active_blocks: int32 [32, 8], P(('grp', 'mem')), may hold values from 0 to 31, as said below
- ridge: float32 [4096], replicated, may hold values from 0.5 to 2
Outputs:
- factored: float32 [8, 128, 128, 128], P('mem', 'grp')
Inputs may be any that keep to these rules, and one draw needn't show every extreme that they name: active_blocks[d, a] % 8 == a for every device d and position a, so a device's blocks are distinct.
All inputs are finite; a program needn't handle non-finite values.
Results may differ from a plain program's by a relative error of at most 0.0003.
Values sent between devices are 32-bit elements; how exact they have to be, the bound alone decides.
No kernel may reach another device: no remote copies, remote signals or barrier semaphores. Data moves between devices by JAX's collectives and lax.ppermute only.
A program may use at most 64 MiB of HBM per device.

v0:
```python
import jax
import jax.numpy as jnp
from jax import lax
from jax.sharding import PartitionSpec as P

NB = 32
BLK = 128
ACT = 8
HI = lax.Precision.HIGHEST


def panel_solve(column):
    count = column.shape[0]
    chol = jnp.linalg.cholesky(column[0])
    stacked = jnp.transpose(column, (2, 0, 1)).reshape(BLK, count * BLK)
    solved = lax.linalg.triangular_solve(chol, stacked, left_side=True, lower=True)
    lower_col = jnp.transpose(solved.reshape(BLK, count, BLK), (1, 2, 0))
    return lower_col.at[0].set(chol)


def apply_step(tiles, lower_col, step, tile_rows, tile_cols):
    left_tiles = jnp.take(lower_col, jnp.maximum(tile_rows - step, 0), axis=0)
    right_tiles = jnp.take(lower_col, jnp.maximum(tile_cols - step, 0), axis=0)
    update = jnp.einsum("tpr,tqr->tpq", left_tiles, right_tiles, precision=HI)
    trailing = ((tile_rows > step) & (tile_cols > step))[:, None, None]
    on_column = ((tile_cols == step) & (tile_rows >= step))[:, None, None]
    on_row = ((tile_rows == step) & (tile_cols > step))[:, None, None]
    tiles = jnp.where(trailing, tiles - update, tiles)
    tiles = jnp.where(on_column, left_tiles, tiles)
    tiles = jnp.where(on_row, jnp.transpose(right_tiles, (0, 2, 1)), tiles)
    return tiles


def column_picker(step, tile_rows, tile_cols):
    wanted = step + jnp.arange(NB - step, dtype=jnp.int32)
    inside = (tile_cols == step) & (tile_rows >= step)
    return ((tile_rows[None, :] == wanted[:, None]) & inside[None, :]).astype(jnp.float32)


def on_device_general(design, active_blocks, ridge):
    n_mem = lax.axis_size("mem")
    n_grp = lax.axis_size("grp")
    member = lax.axis_index("mem")
    group = lax.axis_index("grp")
    classes = n_mem // 8
    per_pos = ACT // classes
    per_row = NB // ACT
    slot_count = NB // classes * per_row
    owned_count = slot_count // n_grp
    row_count = design.shape[0]
    residue = member // 8
    position = member % 8
    everyone = lax.all_gather(active_blocks, "mem", axis=0, tiled=True)
    blocks = design.reshape(row_count, ACT, BLK)
    left = blocks.reshape(row_count, per_pos, classes, BLK)
    outgoing = jnp.einsum("ncqk,nbl->qbckl", left, blocks, preferred_element_type=jnp.float32)
    outgoing = outgoing.reshape(n_mem, per_pos, BLK, BLK)
    received = lax.all_to_all(outgoing, "mem", split_axis=0, concat_axis=0, tiled=True)
    row_ids = jnp.take(everyone.reshape(n_mem, per_pos, classes), residue, axis=2)
    col_ids = jnp.take(everyone, position, axis=1)
    targets = row_ids // classes * per_row + (col_ids // 8)[:, None]
    onehot = (
        targets.reshape(-1)[None, :] == jnp.arange(slot_count, dtype=jnp.int32)[:, None]
    ).astype(jnp.float32)
    sums = jnp.dot(
        onehot,
        received.reshape(n_mem * per_pos, BLK * BLK),
        precision=HI,
        preferred_element_type=jnp.float32,
    )
    sums = sums.reshape(slot_count, BLK, BLK)
    owned = lax.psum_scatter(sums, "grp", scatter_dimension=0, tiled=True)
    slots = group * owned_count + jnp.arange(owned_count, dtype=jnp.int32)
    tile_rows = slots // per_row * classes + residue
    tile_cols = slots % per_row * 8 + position
    ridge_blocks = jnp.take(ridge.reshape(NB, BLK), tile_rows, axis=0)
    same = (tile_rows == tile_cols).astype(jnp.float32)
    extra = jnp.eye(BLK, dtype=jnp.float32)[None] * ridge_blocks[:, None, :] * same[:, None, None]
    divisor = jnp.float32(row_count * n_grp * n_mem // 16)
    tiles = owned / divisor + extra
    picker = column_picker(0, tile_rows, tile_cols)
    partial_value = jnp.einsum("it,tpq->ipq", picker, tiles, precision=HI)
    column = lax.psum(partial_value, ("grp", "mem"))
    lower_col = panel_solve(column)
    tiles = apply_step(tiles, lower_col, 0, tile_rows, tile_cols)
    return tiles[None]


def on_device_fast(design, active_blocks, ridge):
    n_mem = lax.axis_size("mem")
    n_grp = lax.axis_size("grp")
    member = lax.axis_index("mem")
    group = lax.axis_index("grp")
    per_row = NB // ACT
    row_count = design.shape[0]
    divisor = jnp.float32(row_count * n_grp * n_mem // 16)
    eye = jnp.eye(BLK, dtype=jnp.float32)
    ridge_blocks = ridge.reshape(NB, BLK)
    everyone = lax.all_gather(active_blocks, "mem", axis=0, tiled=True)
    blocks = design.reshape(row_count, ACT, BLK)
    outgoing = jnp.einsum("nak,nbl->bakl", blocks, blocks, preferred_element_type=jnp.float32)
    mine00 = jnp.where(active_blocks[0, 0] == 0, outgoing[0, 0], 0.0)
    gram00 = lax.psum(mine00, ("grp", "mem"))
    a00 = gram00 / divisor + eye * ridge_blocks[0][None, :]
    chol = jnp.linalg.cholesky(a00)
    chol_inv = lax.linalg.triangular_solve(chol, eye, left_side=True, lower=True)
    received = lax.all_to_all(outgoing, "mem", split_axis=0, concat_axis=0, tiled=True)
    received = received.reshape(n_mem, ACT, BLK, BLK)
    row_grp = everyone // 8
    col_grp = jnp.take(everyone, member, axis=1) // 8
    grp_ids = jnp.arange(n_grp, dtype=jnp.int32)
    q_ids = jnp.arange(per_row, dtype=jnp.int32)
    mask = (
        (row_grp[:, :, None, None] == grp_ids[None, None, :, None])
        & (col_grp[:, None, None, None] == q_ids[None, None, None, :])
    ).astype(jnp.float32)
    main = jnp.einsum("sagq,sakl->gaqkl", mask, received, precision=HI)
    main = main.reshape(n_grp, ACT * per_row, BLK, BLK)
    col_mask = ((col_grp[:, None] == grp_ids[None, :]) & (everyone[:, 0:1] == 0)).astype(
        jnp.float32
    )
    col_part = jnp.einsum("sg,slk->gkl", col_mask, received[:, 0], precision=HI)
    send = jnp.concatenate([main, col_part[:, None]], axis=1)
    send = send.reshape(n_grp * (ACT * per_row + 1), BLK, BLK)
    got = lax.psum_scatter(send, "grp", scatter_dimension=0, tiled=True)
    owned = got[: ACT * per_row]
    col_tile = got[ACT * per_row] / divisor
    t = jnp.arange(ACT * per_row, dtype=jnp.int32)
    tile_rows = group * 8 + t // per_row
    tile_cols = t % per_row * 8 + member
    same = (tile_rows == tile_cols).astype(jnp.float32)
    diag = eye[None] * jnp.take(ridge_blocks, tile_rows, axis=0)[:, None, :] * same[:, None, None]
    tiles = owned / divisor + diag
    col_rows = lax.all_gather(col_tile, "mem", axis=0, tiled=False)
    col_cols = lax.all_gather(col_tile, "grp", axis=0, tiled=False)
    p_rows = jnp.einsum("ipr,qr->ipq", col_rows, chol_inv, precision=HI)
    p_cols = jnp.einsum("ipr,qr->ipq", col_cols, chol_inv, precision=HI)
    row_ids = group * 8 + jnp.arange(8, dtype=jnp.int32)
    col_ids = jnp.arange(per_row, dtype=jnp.int32) * 8 + member
    p_rows = jnp.where((row_ids == 0)[:, None, None], chol[None], p_rows)
    p_cols = jnp.where((col_ids == 0)[:, None, None], chol[None], p_cols)
    update = jnp.einsum("apr,qsr->aqps", p_rows, p_cols, precision=HI)
    update = update.reshape(ACT * per_row, BLK, BLK)
    left_tiles = jnp.repeat(p_rows, per_row, axis=0)
    right_tiles = jnp.tile(p_cols, (ACT, 1, 1))
    trailing = ((tile_rows > 0) & (tile_cols > 0))[:, None, None]
    on_column = (tile_cols == 0)[:, None, None]
    on_row = ((tile_rows == 0) & (tile_cols > 0))[:, None, None]
    tiles = jnp.where(trailing, tiles - update, tiles)
    tiles = jnp.where(on_column, left_tiles, tiles)
    tiles = jnp.where(on_row, jnp.transpose(right_tiles, (0, 2, 1)), tiles)
    return tiles[None]


def solution(mesh):
    n_mem = mesh.shape["mem"]
    n_grp = mesh.shape["grp"]
    fast = n_mem == 8 and n_grp * 8 == NB
    body = on_device_fast if fast else on_device_general
    in_specs = (P(("grp", "mem"), None), P(("grp", "mem"), None), P())
    out_specs = P("mem", "grp", None, None)
    return jax.shard_map(body, mesh=mesh, in_specs=in_specs, out_specs=out_specs, check_vma=False)
```

profile of v0, /device:TPU:0, one launch (start us, length us, event | category | flops | bytes accessed | tf_op | source)
XLA Modules:
  0.0 329.3 jit_solution(12028579138386191531)
XLA Ops:
  7.4 1.1 copy.56
  8.5 3.8 %convolution_bitcast_fusion.1 = f32[8,8,128,128]{3,2,1,0:T(8,128)} fusion(bf16[256,8,128,1]{2,1,0,3:T(8,128)(2,1)S(1)} %bitcast.82, bf16[256,1024]{1,0:T(8,128)(2,1)} %param.3), kind=kOutput, calls=%fused_computation.5 | convolution fusion | flops 536870912 | bytes 5242880 | tf_op jit(solution)/shard_map/nak,nbl->bakl/dot_general | solution.py:101
  12.3 0.0 copy-start.1
  12.3 5.3 %all-to-all-start = ((f32[8,8,128,128]{3,2,1,0:T(8,128)}), f32[8,8,128,128]{3,2,1,0:T(8,128)}, u32[]{:S(2)}, u32[]{:S(2)}) async-start(f32[8,8,128,128]{3,2,1,0:T(8,128)} %convolution_bitcast_fusion.1), calls=%async_computation | async-start | bytes 8388608 | tf_op jit(solution)/shard_map/all_to_all | solution.py:107
  17.6 0.0 all-reduce.2.cloned.1.call-start
  17.6 0.0 copy-done.1
  17.7 1.5 fusion.10
  19.1 0.0 all-reduce.2.cloned.1.call-update
  19.2 0.0 reduce-scatter.2.cloned.1.call-start
  19.2 50.7 %all-gather = s32[8,1,8]{2,1,0:T(1,128)S(1)} all-gather(s32[1,1,8]{2,1,0:T(1,128)S(1)} %bitcast.87), channel_id=1, replica_groups=mesh['grp'=4,'mem'=8] {'mem'}, dimensions={0}, use_global_device_ids=true | all-gather | bytes 288 | tf_op jit(solution)/shard_map/all_gather | solution.py:99
  69.9 0.1 copy.39
  70.0 0.3 fusion.19
  70.3 0.1 fusion.21
  70.5 0.0 all-to-all-done
  70.5 1.1 slice_bitcast_fusion
  71.6 0.7 convolution_bitcast_fusion.3
  72.2 0.1 copy.43
  72.4 14.0 %convolution_bitcast_fusion = f32[4,8,4,128,128]{4,2,0,3,1:T(4,128)S(1)} fusion(f32[8,8,128,128,1]{3,2,1,0,4:T(8,128)} %bitcast.6, pred[8,4]{0,1:T(4,128)(4,1)S(1)} %iota_compare_fusion.4, pred[8,8,4]{0,2,1:T(4,128)(4,1)S(1)} %iota_compare_fusion.3), kind=kOutput, calls=%fused_computation.2 | convolution fusion | flops 201327616 | bytes 12583200 | tf_op jit(solution)/shard_map/sagq,sakl->gaqkl/dot_general | solution.py:117
  86.4 2.7 copy.41
  89.1 3.9 %pad_maximum_fusion = f32[4,33,128,128]{3,2,1,0:T(8,128)} fusion(f32[4,1,128,128]{3,2,1,0:T(8,128)S(1)} %copy.43, f32[4,32,128,128]{3,2,1,0:T(8,128)S(1)} %bitcast.80), kind=kLoop, calls=%fused_computation.1 | loop fusion | flops 2162688 | bytes 17301504 | tf_op jit(solution)/shard_map/concatenate | solution.py:123
  93.0 0.0 copy-start
  93.0 0.0 reduce-scatter.2.cloned.1.call-update
  93.1 0.7 copy-done
  93.8 0.6 gather_fusion
  94.4 0.1 broadcast_select_fusion
  94.5 167.3 %all-reduce.2.cloned.1.call-done = f32[128,128]{1,0:T(8,128)} async-done(((f32[128,128]{1,0:T(8,128)}), f32[128,128]{1,0:T(8,128)}) %all-reduce.2.cloned.1.call-update) | async-done | bytes 65552 | tf_op jit(solution)/shard_map/psum | solution.py:103
  261.8 0.9 select_add_fusion
  262.7 0.1 copy.38
  262.8 0.9 fusion.12
  263.7 11.7 %cholesky.23 = f32[128,128]{1,0:T(8,128)S(1)} custom-call(f32[128,128]{1,0:T(8,128)S(1)} %fusion.12), custom_call_target="Cholesky" | custom-call | tf_op jit(solution)/shard_map/jit(cholesky)/cholesky | solution.py:105
  275.4 0.6 compare_reduce_fusion
  276.1 0.7 select_bitcast_fusion
  276.7 9.8 %custom-call.6 = f32[1,128,128]{1,2,0:T(8,128)S(1)} custom-call(f32[1,128,128]{2,1,0:T(8,128)S(1)} %get-tuple-element.16), custom_call_target="InvertDiagBlocksLowerTriangular" | custom-call | tf_op jit(solution)/shard_map/triangular_solve | solution.py:106
  286.5 0.2 convolution_bitcast_fusion.4
  286.8 0.0 reduce-scatter.2.cloned.1.call-done
  286.8 0.8 slice_multiply_fusion.1
  287.7 15.1 %all_gather.12 = f32[4,128,128]{2,1,0:T(8,128)S(1)} all-gather(f32[1,128,128]{2,1,0:T(8,128)S(1)} %slice_multiply_fusion.1), channel_id=1, replica_groups=mesh['grp'=4,'mem'=8] {'grp'}, dimensions={0}, use_global_device_ids=true | all-gather | bytes 327680 | tf_op jit(solution)/shard_map/all_gather | solution.py:135
  302.8 10.0 %all_gather.13 = f32[8,128,128]{2,1,0:T(8,128)S(1)} all-gather(f32[1,128,128]{2,1,0:T(8,128)S(1)} %slice_multiply_fusion.1), channel_id=1, replica_groups=mesh['grp'=4,'mem'=8] {'mem'}, dimensions={0}, use_global_device_ids=true | all-gather | bytes 589824 | tf_op jit(solution)/shard_map/all_gather | solution.py:134
  312.8 0.4 convolution_select_fusion.1
  313.2 0.1 copy.44
  313.3 0.6 convolution_select_fusion
  313.9 1.8 convolution_bitcast_fusion.2
  315.7 1.9 copy.45
  317.6 4.3 %fusion.3 = f32[1,32,128,128]{3,2,1,0:T(8,128)} fusion(f32[33,128,128]{2,1,0:T(8,128)} %reduce-scatter.2.cloned.1.call-done, f32[8,4,128,128]{3,2,1,0:T(8,128)} %copy.45, f32[32]{0:T(128)S(1)} %get-tuple-element.18, f32[32,128]{1,0:T(8,128)S(1)} %broadcast_select_fusion, f32[128,128]{1,0:T(8,128)S(1)} %fusion.13, ...), kind=kLoop, calls=%fused_computation.8 | loop fusion | flops 4194304 | bytes 7160032 | tf_op jit(solution)/shard_map/broadcast_in_dim | solution.py:152
  (14 shorter events, 0.1 us)
Async XLA Ops:
  12.3 5.3 %copy-start.1 = (s32[1,8]{1,0:T(1,128)S(1)}, s32[1,8]{1,0:T(1,128)}, u32[]{:S(2)}) copy-start(s32[1,8]{1,0:T(1,128)} %param.4) | copy-start | bytes 100
  12.3 58.2 %all-to-all-start = ((f32[8,8,128,128]{3,2,1,0:T(8,128)}), f32[8,8,128,128]{3,2,1,0:T(8,128)}, u32[]{:S(2)}, u32[]{:S(2)}) async-start(f32[8,8,128,128]{3,2,1,0:T(8,128)} %convolution_bitcast_fusion.1), calls=%async_computation | async-start | bytes 8388608 | tf_op jit(solution)/shard_map/all_to_all | solution.py:107
  17.6 244.3 %all-reduce.2.cloned.1.call-start = ((), (), s32[]{:S(2)}) async-start(), calls=%async_computation.2 | async-start | bytes 131072 | tf_op jit(solution)/shard_map/psum | solution.py:103
  19.2 267.6 %reduce-scatter.2.cloned.1.call-start = ((), (), s32[]{:S(2)}) async-start(), calls=%async_computation.3 | async-start | bytes 10813440 | tf_op jit(solution)/shard_map/reduce_scatter | solution.py:125
  93.0 0.7 copy-start
Sparse Core Ops, SparseCore 0:
  24.0 237.8 all-reduce.1
Sparse Core Ops, SparseCore 1:
  93.1 149.5 reduce-scatter.1
where the time goes:
time: 330 us; the launch traced here: 329 us
  waiting for transfers between devices  167 us (51%)
  blocking collectives  75.8 us (23%)
  other arithmetic  35.7 us (11%)
  matrix products  21.5 us (7%)
  between operations  15.1 us (5%)
  local copies, waits for them, and re-layouts  8.48 us (3%)
  starting transfers between devices  5.37 us (2%)
    psum x1, waiting for transfers between devices, on_device_fast(): gram00 = lax.psum(mine00, ('grp', 'mem'))  167 us
    all_gather x1, blocking collectives, on_device_fast(): everyone = lax.all_gather(active_blocks, 'mem', axis=0, tiled=True)  50.7 us
    all_gather x1, blocking collectives, on_device_fast(): col_cols = lax.all_gather(col_tile, 'grp', axis=0, tiled=False)  15.1 us
    dot_general x1, matrix products, on_device_fast(): main = jnp.einsum('sagq,sakl->gaqkl', mask, received, precision=HI)  14 us
    another operation x3, other arithmetic, on_device_fast(): chol = jnp.linalg.cholesky(a00)  12.4 us
    another operation x2, other arithmetic, on_device_fast(): lax.linalg.triangular_solve(chol, eye, left_side=True, lower=True)  10.5 us
    all_gather x1, blocking collectives, on_device_fast(): col_rows = lax.all_gather(col_tile, 'mem', axis=0, tiled=False)  10 us
  transfers between devices with their start and end apart: 3, of which 1 were waited for; matrix products, arithmetic and copies ran while one was open for 15% of the time, Pallas kernels for 0%

commit v1 on v0

--- a/solution.py
+++ b/solution.py
@@ -100,7 +100,7 @@
     blocks = design.reshape(row_count, ACT, BLK)
     outgoing = jnp.einsum("nak,nbl->bakl", blocks, blocks, preferred_element_type=jnp.float32)
     mine00 = jnp.where(active_blocks[0, 0] == 0, outgoing[0, 0], 0.0)
-    gram00 = lax.psum(mine00, ("grp", "mem"))
+    gram00 = jnp.sum(lax.all_gather(mine00, ("grp", "mem")), axis=0)
     a00 = gram00 / divisor + eye * ridge_blocks[0][None, :]
     chol = jnp.linalg.cholesky(a00)
     chol_inv = lax.linalg.triangular_solve(chol, eye, left_side=True, lower=True)

time: 330 us -> 287 us (0.87)
  waiting for transfers between devices: 167 us -> 123 us
  local copies, waits for them, and re-layouts: 8.48 us -> 14.9 us
  matrix products: 21.5 us -> 16.4 us
    psum x1 -> x0, waiting for transfers between devices: 167 us -> none  [on_device_fast(): gram00 = lax.psum(mine00, ('grp', 'mem'))]
    reduce_scatter x1, waiting for transfers between devices: 0.03 us -> 123 us  [on_device_fast(): got = lax.psum_scatter(send, 'grp', scatter_dimension=0, tiled=True)]
    all_to_all x0 -> x1, local copies, waits for them, and re-layouts: none -> 5.36 us  [on_device_fast(): lax.all_to_all(outgoing, 'mem', split_axis=0, concat_axis=0, tiled=True)]
    dot_general x1, matrix products: 14 us -> 9.26 us  [on_device_fast(): main = jnp.einsum('sagq,sakl->gaqkl', mask, received, precision=HI)]
  transfers between devices with their start and end apart: 3 -> 3, of which waited for: 1 -> 1; matrix products, arithmetic and copies ran while one was open for 15% -> 18% of each run, Pallas kernels for 0% -> 0%
where the time goes in v1:
time: 287 us
  waiting for transfers between devices  123 us (43%)
  blocking collectives  76.4 us (27%)
  other arithmetic  35.1 us (12%)
  matrix products  16.4 us (6%)
  between operations  15.1 us (5%)
  local copies, waits for them, and re-layouts  14.9 us (5%)
  starting transfers between devices  5.38 us (2%)
    reduce_scatter x1, waiting for transfers between devices, on_device_fast(): got = lax.psum_scatter(send, 'grp', scatter_dimension=0, tiled=True)  123 us
    all_gather x1, blocking collectives, on_device_fast(): everyone = lax.all_gather(active_blocks, 'mem', axis=0, tiled=True)  51.8 us
    all_gather x1, blocking collectives, on_device_fast(): col_cols = lax.all_gather(col_tile, 'grp', axis=0, tiled=False)  14.6 us
    another operation x3, other arithmetic, on_device_fast(): chol = jnp.linalg.cholesky(a00)  12.4 us
    another operation x2, other arithmetic, on_device_fast(): lax.linalg.triangular_solve(chol, eye, left_side=True, lower=True)  10.5 us
    all_gather x1, blocking collectives, on_device_fast(): col_rows = lax.all_gather(col_tile, 'mem', axis=0, tiled=False)  10 us
    dot_general x1, matrix products, on_device_fast(): main = jnp.einsum('sagq,sakl->gaqkl', mask, received, precision=HI)  9.26 us
  transfers between devices with their start and end apart: 3, of which 1 were waited for; matrix products, arithmetic and copies ran while one was open for 18% of the time, Pallas kernels for 0%

profile of v1, /device:TPU:0, one launch (start us, length us, event | category | flops | bytes accessed | tf_op | source)
XLA Modules:
  0.0 286.6 jit_solution(6870392667282310443)
XLA Ops:
  7.4 1.1 copy.65
  8.5 3.8 %convolution_bitcast_fusion.1 = f32[8,8,128,128]{2,3,1,0:T(8,128)} fusion(bf16[256,8,128,1]{2,1,0,3:T(8,128)(2,1)S(1)} %bitcast.84, bf16[256,1024]{1,0:T(8,128)(2,1)} %param.3), kind=kOutput, calls=%fused_computation.4 | convolution fusion | flops 536870912 | bytes 5242880 | tf_op jit(solution)/shard_map/nak,nbl->bakl/dot_general | solution.py:101
  12.3 0.0 copy-start.1
  12.3 5.3 %all-to-all-start = ((f32[8,8,128,128]{2,3,1,0:T(8,128)}), f32[8,8,128,128]{2,3,1,0:T(8,128)}, u32[]{:S(2)}, u32[]{:S(2)}) async-start(f32[8,8,128,128]{2,3,1,0:T(8,128)} %convolution_bitcast_fusion.1), calls=%async_computation | async-start | bytes 8388608 | tf_op jit(solution)/shard_map/all_to_all | solution.py:107
  17.6 0.0 all-gather.4.cloned.1.call-start
  17.6 0.0 copy-done.1
  17.7 0.8 slice_select_fusion
  18.5 0.7 copy.46
  19.2 0.0 all-gather.4.cloned.1.call-update
  19.3 0.0 reduce-scatter.2.cloned.1.call-start
  19.3 51.8 %all-gather.1 = s32[8,1,8]{2,1,0:T(1,128)S(1)} all-gather(s32[1,1,8]{2,1,0:T(1,128)S(1)} %bitcast.89), channel_id=1, replica_groups=mesh['grp'=4,'mem'=8] {'mem'}, dimensions={0}, use_global_device_ids=true | all-gather | bytes 288 | tf_op jit(solution)/shard_map/all_gather | solution.py:99
  71.1 0.1 copy.49
  71.2 0.3 fusion.17
  71.5 0.1 fusion.19
  71.7 0.0 all-to-all-done
  71.7 1.1 slice_bitcast_fusion
  72.8 0.2 copy.52
  73.0 0.4 convolution_bitcast_fusion.3
  73.4 0.1 copy.53
  73.5 5.4 %copy.57 = f32[8,8,128,128,1]{3,0,4,2,1:T(8,128)} copy(f32[8,8,128,128,1]{2,3,1,0,4:T(8,128)} %bitcast.5) | data formatting | bytes 8388608 | tf_op jit(solution)/shard_map/all_to_all | solution.py:107
  78.9 9.3 %convolution_bitcast_fusion = f32[4,8,4,128,128]{4,2,0,3,1:T(4,128)S(1)} fusion(f32[8,8,128,128,1]{3,0,4,2,1:T(8,128)} %copy.57, pred[8,4]{0,1:T(4,128)(4,1)S(1)} %iota_compare_fusion.5, pred[8,8,4]{0,2,1:T(4,128)(4,1)S(1)} %iota_compare_fusion.4), kind=kOutput, calls=%fused_computation.2 | convolution fusion | flops 201327616 | bytes 12583200 | tf_op jit(solution)/shard_map/sagq,sakl->gaqkl/dot_general | solution.py:117
  88.1 2.7 copy.51
  90.8 3.9 %pad_maximum_fusion = f32[4,33,128,128]{3,2,1,0:T(8,128)} fusion(f32[4,1,128,128]{3,2,1,0:T(8,128)S(1)} %copy.53, f32[4,32,128,128]{3,2,1,0:T(8,128)S(1)} %bitcast.82), kind=kLoop, calls=%fused_computation.1 | loop fusion | flops 2162688 | bytes 17301504 | tf_op jit(solution)/shard_map/concatenate | solution.py:123
  94.8 0.0 copy-start
  94.8 0.0 reduce-scatter.2.cloned.1.call-update
  94.8 0.7 copy-done
  95.5 0.6 gather_fusion
  96.2 0.1 broadcast_select_fusion
  96.2 0.0 all-gather.4.cloned.1.call-done
  96.2 1.7 reduce_sum.9
  97.9 0.1 copy.47
  98.1 0.1 copy.48
  98.2 0.1 fusion.10
  98.2 11.7 %cholesky.23 = f32[128,128]{1,0:T(8,128)S(1)} custom-call(f32[128,128]{1,0:T(8,128)S(1)} %fusion.10), custom_call_target="Cholesky" | custom-call | tf_op jit(solution)/shard_map/jit(cholesky)/cholesky | solution.py:105
  110.0 0.6 compare_reduce_fusion
  110.6 0.7 select_bitcast_fusion
  111.3 9.8 %custom-call.6 = f32[1,128,128]{1,2,0:T(8,128)S(1)} custom-call(f32[1,128,128]{2,1,0:T(8,128)S(1)} %get-tuple-element.16), custom_call_target="InvertDiagBlocksLowerTriangular" | custom-call | tf_op jit(solution)/shard_map/triangular_solve | solution.py:106
  121.1 0.2 convolution_bitcast_fusion.4
  121.4 123.3 %reduce-scatter.2.cloned.1.call-done = f32[33,128,128]{2,1,0:T(8,128)} async-done(((f32[132,128,128]{2,1,0:T(8,128)}), f32[33,128,128]{2,1,0:T(8,128)}) %reduce-scatter.2.cloned.1.call-update) | async-done | bytes 2162704 | tf_op jit(solution)/shard_map/reduce_scatter | solution.py:125
  244.7 0.8 slice_multiply_fusion.1
  245.5 14.6 %all_gather.17 = f32[4,128,128]{2,1,0:T(8,128)S(1)} all-gather(f32[1,128,128]{2,1,0:T(8,128)S(1)} %slice_multiply_fusion.1), channel_id=1, replica_groups=mesh['grp'=4,'mem'=8] {'grp'}, dimensions={0}, use_global_device_ids=true | all-gather | bytes 327680 | tf_op jit(solution)/shard_map/all_gather | solution.py:135
  260.1 10.0 %all_gather.18 = f32[8,128,128]{2,1,0:T(8,128)S(1)} all-gather(f32[1,128,128]{2,1,0:T(8,128)S(1)} %slice_multiply_fusion.1), channel_id=1, replica_groups=mesh['grp'=4,'mem'=8] {'mem'}, dimensions={0}, use_global_device_ids=true | all-gather | bytes 589824 | tf_op jit(solution)/shard_map/all_gather | solution.py:134
  270.1 0.4 convolution_select_fusion.1
  270.5 0.1 copy.54
  270.7 0.6 convolution_select_fusion
  271.2 1.8 convolution_bitcast_fusion.2
  273.0 1.9 copy.55
  274.9 4.3 %fusion.2 = f32[1,32,128,128]{3,2,1,0:T(8,128)} fusion(f32[33,128,128]{2,1,0:T(8,128)} %reduce-scatter.2.cloned.1.call-done, f32[8,4,128,128]{3,2,1,0:T(8,128)} %copy.55, f32[32]{0:T(128)S(1)} %get-tuple-element.18, f32[32,128]{1,0:T(8,128)S(1)} %broadcast_select_fusion, f32[128,128]{1,0:T(8,128)S(1)} %fusion.11, ...), kind=kLoop, calls=%fused_computation.7 | loop fusion | flops 4194304 | bytes 7160032 | tf_op jit(solution)/shard_map/broadcast_in_dim | solution.py:152
  (15 shorter events, 0.2 us)
Async XLA Ops:
  12.3 5.3 %copy-start.1 = (s32[1,8]{1,0:T(1,128)S(1)}, s32[1,8]{1,0:T(1,128)}, u32[]{:S(2)}) copy-start(s32[1,8]{1,0:T(1,128)} %param.4) | copy-start | bytes 100
  12.3 59.4 %all-to-all-start = ((f32[8,8,128,128]{2,3,1,0:T(8,128)}), f32[8,8,128,128]{2,3,1,0:T(8,128)}, u32[]{:S(2)}, u32[]{:S(2)}) async-start(f32[8,8,128,128]{2,3,1,0:T(8,128)} %convolution_bitcast_fusion.1), calls=%async_computation | async-start | bytes 8388608 | tf_op jit(solution)/shard_map/all_to_all | solution.py:107
  17.6 78.7 %all-gather.4.cloned.1.call-start = ((), (), s32[]{:S(2)}) async-start(), calls=%async_computation.3 | async-start | bytes 2162688 | tf_op jit(solution)/shard_map/all_gather | solution.py:103
  19.3 225.4 %reduce-scatter.2.cloned.1.call-start = ((), (), s32[]{:S(2)}) async-start(), calls=%async_computation.2 | async-start | bytes 10813440 | tf_op jit(solution)/shard_map/reduce_scatter | solution.py:125
  94.8 0.7 copy-start
Sparse Core Ops, SparseCore 0:
  21.3 69.3 all-gather.3
Sparse Core Ops, SparseCore 1:
  94.9 149.7 reduce-scatter.1
